TPU v7x, 256 devices: a whole 4x4x8 slice. The times are simulated.
256 devices in a mesh: query: 8 (over x, core), bank: 32 (over z, y).
Axes of the slice: x: 4, y: 4, z: 8, core: 2. Of those that a mesh axis runs over, the one named last changes fastest.
Arguments:
- queries: bfloat16 [2048, 32, 128], P(('query', 'bank'))
- passages: bfloat16 [8192, 128, 128], P('bank')
- passage_home: int32 [8192], replicated, may hold values from 0 to 8191, as said below
- candidates: int32 [2048, 16], P(('query', 'bank')), may hold values from 0 to 8191, as said below
- positive: int32 [2048], P(('query', 'bank')), may hold values from 0 to 15
Outputs:
- losses: float32 [2048], P(('query', 'bank'))
- query_grads: float32 [2048, 32, 128], P(('query', 'bank'))
Inputs may be any that keep to these rules, and one draw needn't show every extreme that they name: `passage_home`: each passage id has its own storage row; storage row r lies on bank index r // 256. `candidates`: among the 128 list entries of one device's queries (aligned blocks of 8 queries, in order), at most 12 name passages stored on one bank index; in every block some bank index gets exactly 12, and in each group of 32 consecutive blocks it is the same bank index for all of them.
All inputs are finite; a program needn't handle non-finite values.
Results may differ from a plain program's by a relative error of at most 0.0049.
Values may be sent and summed in bfloat16 or wider, within the bound.
No kernel may reach another device: no remote copies, remote signals or barrier semaphores. Data moves between devices by JAX's collectives and lax.ppermute only.
A program may use at most 128 MiB of HBM per device.

v0:
```python
import jax
import jax.numpy as jnp
import numpy as np
from jax import lax
from jax.sharding import Mesh
from jax.sharding import PartitionSpec as P

BANK = ("z", "y")


def soft_terms(scores):
    largest = jnp.max(scores, axis=-1, keepdims=True)
    raised = jnp.exp(scores - largest)
    totals = jnp.sum(raised, axis=-1, keepdims=True)
    maxima = largest[..., 0] + jnp.log(totals[..., 0])
    weights = (raised / totals).astype(jnp.bfloat16)
    return (maxima, weights)


def contrast(similarity, positive):
    largest = jnp.max(similarity, axis=1, keepdims=True)
    raised = jnp.exp(similarity - largest)
    totals = jnp.sum(raised, axis=1, keepdims=True)
    picked = jnp.arange(similarity.shape[1], dtype=jnp.int32)[None, :] == positive[:, None]
    losses = (
        largest[:, 0] + jnp.log(totals[:, 0]) - jnp.sum(jnp.where(picked, similarity, 0.0), axis=1)
    )
    coefficients = (raised / totals - picked.astype(jnp.float32)).astype(jnp.bfloat16)
    return (losses, coefficients)


def split3(value):
    high = lax.reduce_precision(value, exponent_bits=8, mantissa_bits=7)
    rest = value - high
    middle = lax.reduce_precision(rest, exponent_bits=8, mantissa_bits=7)
    low = rest - middle
    return jnp.stack([high, middle, low], axis=-1).astype(jnp.bfloat16)


def join3(pieces):
    pieces = pieces.astype(jnp.float32)
    return pieces[..., 0] + pieces[..., 1] + pieces[..., 2]


def gather_bank(value):
    value = lax.all_gather(value, "y", axis=0, tiled=True)
    return lax.all_gather(value, "z", axis=0, tiled=True)


def body(queries, passages, passage_home, candidates, positive):
    shards = lax.axis_size(BANK)
    me = lax.axis_index(BANK)
    query_rows, query_len, feature_dim = queries.shape
    listed = candidates.shape[1]
    holdings = passages.shape[0]
    entries = query_rows * listed
    capacity = 3 * entries // shards
    width = query_len * feature_dim
    tail = 128
    lists = jnp.concatenate([candidates, positive[:, None]], axis=1)
    group_candidates = gather_bank(lists)[:, :listed]
    group_queries = gather_bank(queries)
    storage = passage_home[group_candidates].reshape(shards, entries)
    mine = storage // holdings == me
    position = jnp.cumsum(mine.astype(jnp.int32), axis=1) - 1
    slot_ids = jnp.arange(capacity, dtype=jnp.int32)
    hit = mine[:, None, :] & (position[:, None, :] == slot_ids[None, :, None])
    entry_ids = jnp.arange(entries, dtype=jnp.int32)
    entry = jnp.sum(jnp.where(hit, entry_ids[None, None, :], 0), axis=2)
    local_slot = jnp.sum(jnp.where(hit, (storage % holdings)[:, None, :], 0), axis=2)
    source = jnp.arange(shards, dtype=jnp.int32)[:, None]
    query_index = (source * query_rows + entry // listed).reshape(-1)
    local_slot = local_slot.reshape(-1)
    passage_tiles = passages[local_slot]
    query_tiles = group_queries[query_index]
    scores = jnp.einsum(
        "sid,sjd->sij", query_tiles, passage_tiles, preferred_element_type=jnp.float32
    )
    maxima, weights = soft_terms(scores)
    token_basis = jnp.einsum(
        "sij,sjd->sid", weights, passage_tiles, preferred_element_type=jnp.float32
    ).astype(jnp.bfloat16)
    slot_similarity = split3(jnp.sum(maxima, axis=1)).reshape(shards, capacity * 3)
    payload = jnp.concatenate(
        [
            token_basis.reshape(shards, capacity * width),
            slot_similarity,
            jnp.zeros((shards, tail - capacity * 3), jnp.bfloat16),
        ],
        axis=1,
    )
    returned = lax.all_to_all(payload, BANK, 0, 0, tiled=True)
    own_storage = passage_home[candidates].reshape(entries)
    holder = own_storage // holdings
    member = holder[:, None] == jnp.arange(shards, dtype=jnp.int32)[None, :]
    member = member.astype(jnp.int32)
    own_position = jnp.sum((jnp.cumsum(member, axis=0) - member) * member, axis=1)
    pieces = returned[:, capacity * width : capacity * width + capacity * 3]
    pieces = pieces.reshape(shards * capacity, 3)
    flat_slot = holder * capacity + own_position
    similarity = join3(pieces[flat_slot]).reshape(query_rows, listed)
    losses, coefficients = contrast(similarity, positive)
    slot_of = flat_slot.reshape(query_rows, listed)
    spread = jnp.arange(shards * capacity, dtype=jnp.int32)[None, None, :] == slot_of[:, :, None]
    spread = jnp.sum(
        jnp.where(spread, coefficients[:, :, None].astype(jnp.float32), 0.0), axis=1
    ).astype(jnp.bfloat16)
    bases = returned[:, : capacity * width].reshape(shards * capacity, width)
    gradient = jnp.einsum("qs,sd->qd", spread, bases, preferred_element_type=jnp.float32)
    return (losses, gradient.reshape(query_rows, query_len, feature_dim))


def solution(mesh):
    rows = mesh.shape["query"]
    bank = mesh.shape["bank"]
    across = 4 if bank % 4 == 0 else 1
    devices = np.asarray(mesh.devices).reshape(rows, bank // across, across)
    split_mesh = Mesh(devices, ("query",) + BANK)
    every = ("query",) + BANK
    return jax.shard_map(
        body,
        mesh=split_mesh,
        in_specs=(P(every, None, None), P(BANK, None, None), P(), P(every, None), P(every)),
        out_specs=(P(every), P(every, None, None)),
        check_vma=False,
    )
```

profile of v0, /device:TPU:2, one launch (start us, length us, event | category | flops | bytes accessed | tf_op | source)
XLA Modules:
  0.0 256.7 jit_solution(14263057151190145409)
XLA Ops:
  7.2 14.5 %all_gather.12 = bf16[32,32,128]{2,1,0:T(8,128)(2,1)} all-gather(bf16[8,32,128]{2,1,0:T(8,128)(2,1)} %param.5), channel_id=1, replica_groups=mesh['query'=8,'z'=8,'y'=4] {'y'}, dimensions={0}, use_global_device_ids=true | all-gather | bytes 327680 | tf_op jit(solution)/shard_map/all_gather | solution.py:46
  21.7 0.7 copy.33
  22.4 0.8 pad_add_fusion
  23.2 12.0 %all_gather.14 = s32[32,17]{1,0:T(8,128)S(1)} all-gather(s32[8,17]{1,0:T(8,128)S(1)} %pad_add_fusion), channel_id=1, replica_groups=mesh['query'=8,'z'=8,'y'=4] {'y'}, dimensions={0}, use_global_device_ids=true | all-gather | bytes 2720 | tf_op jit(solution)/shard_map/all_gather | solution.py:46
  35.3 28.2 %all-gather = s32[8,32,17]{1,2,0:T(8,128)S(1)} all-gather(s32[1,32,17]{1,2,0:T(8,128)S(1)} %copy.34), channel_id=1, replica_groups=mesh['query'=8,'z'=8,'y'=4] {'z'}, dimensions={0}, use_global_device_ids=true | all-gather | bytes 19584 | tf_op jit(solution)/shard_map/all_gather | solution.py:47
  63.9 23.0 %gather_fusion = s32[4096]{0:T(1024)S(1)} fusion(s32[8192]{0:T(1024)S(1)} %copy-done, s32[4096]{0:T(1024)S(1)} %broadcast_clamp_fusion), kind=kCustom, calls=%fused_computation | custom fusion | bytes 49152 | tf_op jit(solution)/shard_map/gather | solution.py:63
  88.4 14.4 %gather_fusion.2 = bf16[384,128,128]{2,1,0:T(8,128)(2,1)} fusion(bf16[256,128,128]{2,1,0:T(8,128)(2,1)} %param.6, s32[1024]{0:T(1024)S(1)} %pad_clamp_fusion.2), kind=kCustom, calls=%fused_computation.2 | custom fusion | bytes 25167360 | tf_op jit(solution)/shard_map/gather | solution.py:74
  102.9 2.8 %gather_fusion.1 = bf16[384,32,128]{2,1,0:T(8,128)(2,1)S(1)} fusion(bf16[256,32,128]{2,1,0:T(8,128)(2,1)} %all-gather.3.cloned.1.call-done, s32[1024]{0:T(1024)S(1)} %pad_clamp_fusion.3), kind=kCustom, calls=%fused_computation.1 | custom fusion | bytes 6292992 | tf_op jit(solution)/shard_map/gather | solution.py:75
  105.7 11.3 %fusion.27 = (f32[384,32]{1,0:T(8,128)S(1)}, f32[384,32,128]{2,1,0:T(8,128)}) fusion(bf16[384,32,128]{2,1,0:T(8,128)(2,1)S(1)} %gather_fusion.1, bf16[384,128,128]{2,1,0:T(8,128)(2,1)} %gather_fusion.2), kind=kOutput, calls=%fused_computation.94 | convolution fusion | flops 404213760 | bytes 22069248 | tf_op jit(solution)/shard_map/sid,sjd->sij/dot_general | solution.py:76
  117.0 5.8 %fusion = f32[384,32]{1,0:T(8,128)S(1)} fusion(f32[384,32,128]{2,1,0:T(8,128)} %get-tuple-element.24, f32[384,32]{1,0:T(8,128)S(1)} %get-tuple-element.23), kind=kLoop, calls=%fused_computation.7 | loop fusion | flops 3133440 | bytes 6389760 | tf_op jit(solution)/shard_map/reduce_sum | solution.py:14
  122.9 7.1 %fusion.4 = bf16[384,32,128]{2,1,0:T(8,128)(2,1)S(1)} fusion(bf16[384,128,128]{2,1,0:T(8,128)(2,1)} %gather_fusion.2, f32[384,32,128]{2,1,0:T(8,128)S(1)} %copy-done.1, f32[384,32]{1,0:T(8,128)S(1)} %fusion, f32[384,32]{1,0:T(8,128)S(1)} %get-tuple-element.23), kind=kOutput, calls=%fused_computation.12 | convolution fusion | flops 408944640 | bytes 22118400 | tf_op jit(solution)/shard_map/sij,sjd->sid/dot_general | solution.py:80
  130.2 2.8 %reshape.480 = bf16[32,49152]{1,0:T(8,128)(2,1)} reshape(bf16[384,32,128]{2,1,0:T(8,128)(2,1)S(1)} %fusion.4) | data formatting | bytes 6291456 | tf_op jit(solution)/shard_map/reshape | solution.py:86
  133.0 2.1 constant_dynamic-update-slice_fusion
  136.0 1.7 copy-done.2
  138.1 5.0 %reduce.6 = bf16[32,49280]{1,0:T(8,128)(2,1)S(1)} reduce(bf16[32,1,49280]{2,0,1:T(8,128)(2,1)} %bitcast.63, bf16[]{:T(256)} %broadcast.445), dimensions={1}, to_apply=%copy.40.reduce_sub_computation | reduce | bytes 6307842 | tf_op jit(solution)/shard_map/all_to_all | solution.py:92
  143.1 3.6 %reshape.538 = bf16[32,2,24640]{2,1,0:T(2,128)(2,1)} reshape(bf16[32,49280]{1,0:T(8,128)(2,1)S(1)} %reduce.6) | data formatting | bytes 6307840
  146.7 6.5 %all-to-all-start = ((bf16[32,2,24640]{2,1,0:T(2,128)(2,1)}), bf16[32,2,24640]{2,1,0:T(2,128)(2,1)S(1)}, u32[]{:S(2)}, u32[]{:S(2)}) async-start(bf16[32,2,24640]{2,1,0:T(2,128)(2,1)} %reshape.538), calls=%async_computation | async-start | bytes 6324224 | tf_op jit(solution)/shard_map/all_to_all | solution.py:92
  153.4 1.1 gather_fusion.3
  155.2 62.0 %all-to-all-done = bf16[32,2,24640]{2,1,0:T(2,128)(2,1)S(1)} async-done(((bf16[32,2,24640]{2,1,0:T(2,128)(2,1)}), bf16[32,2,24640]{2,1,0:T(2,128)(2,1)S(1)}, u32[]{:S(2)}, u32[]{:S(2)}) %all-to-all-start) | async-done | bytes 3153952 | tf_op jit(solution)/shard_map/all_to_all | solution.py:92
  217.2 16.4 %reshape.539 = bf16[32,1,49280]{2,1,0:T(2,128)(2,1)} reshape(bf16[32,2,24640]{2,1,0:T(2,128)(2,1)S(1)} %all-to-all-done) | data formatting | bytes 6307840
  233.5 3.1 %copy.45 = bf16[32,1,49280]{2,0,1:T(8,128)(2,1)S(1)} copy(bf16[32,1,49280]{2,1,0:T(2,128)(2,1)} %reshape.539) | data formatting | bytes 6307840
  239.0 5.7 %reshape.484 = bf16[384,4096]{1,0:T(8,128)(2,1)} reshape(bf16[32,49152]{1,0:T(8,128)(2,1)S(1)} %slice.39) | data formatting | bytes 6291456 | tf_op jit(solution)/shard_map/reshape | solution.py:108
  244.7 3.4 %copy.41 = bf16[384,4096]{0,1:T(8,128)(2,1)S(1)} copy(bf16[384,4096]{1,0:T(8,128)(2,1)} %reshape.484) | data formatting | bytes 6291456 | tf_op jit(solution)/shard_map/reshape | solution.py:108
  248.2 0.9 fusion.12
  (68 shorter events, 7.2 us)
Async XLA Ops:
  7.2 56.7 %copy-start = (s32[8192]{0:T(1024)S(1)}, s32[8192]{0:T(1024)}, u32[]{:S(2)}) copy-start(s32[8192]{0:T(1024)} %param.7) | copy-start | bytes 98308
  7.2 95.7 %all-gather.3.cloned.1.call-start = ((), (), s32[]{:S(2)}) async-start(), calls=%async_computation.1 | async-start | bytes 2359296 | tf_op jit(solution)/shard_map/all_gather | solution.py:47
  117.0 5.8 %copy-start.1 = (f32[384,32,128]{2,1,0:T(8,128)S(1)}, f32[384,32,128]{2,1,0:T(8,128)}, u32[]{:S(2)}) copy-start(f32[384,32,128]{2,1,0:T(8,128)} %get-tuple-element.24) | copy-start | bytes 18874372
  135.9 1.7 copy-start.2
  146.7 6.5 %copy-start.3 = (s32[8,16]{1,0:T(8,128)S(1)}, s32[8,16]{1,0:T(8,128)}, u32[]{:S(2)}) copy-start(s32[8,16]{1,0:T(8,128)} %param.8) | copy-start | bytes 1540
  146.7 70.4 %all-to-all-start = ((bf16[32,2,24640]{2,1,0:T(2,128)(2,1)}), bf16[32,2,24640]{2,1,0:T(2,128)(2,1)S(1)}, u32[]{:S(2)}, u32[]{:S(2)}) async-start(bf16[32,2,24640]{2,1,0:T(2,128)(2,1)} %reshape.538), calls=%async_computation | async-start | bytes 6324224 | tf_op jit(solution)/shard_map/all_to_all | solution.py:92
  236.7 1.5 copy-start.4
Sparse Core Ops, SparseCore 0:
  21.8 42.7 all-gather.2
where the time goes:
time: 257 us
  local copies, waits for them, and re-layouts  85.3 us (33%)
  waiting for transfers between devices  62 us (24%)
  blocking collectives  54.7 us (21%)
  matrix products  19.4 us (8%)
  other arithmetic  14.4 us (6%)
  between operations  14.4 us (6%)
  starting transfers between devices  6.57 us (3%)
    all_to_all x1, waiting for transfers between devices, body(): returned = lax.all_to_all(payload, BANK, 0, 0, tiled=True)  62 us
    all_gather x1, blocking collectives, gather_bank(): return lax.all_gather(value, 'z', axis=0, tiled=True)  28.2 us
    unnamed x18, local copies, waits for them, and re-layouts  27.9 us
    all_gather x2, blocking collectives, gather_bank(): value = lax.all_gather(value, 'y', axis=0, tiled=True)  26.5 us
    gather x1, local copies, waits for them, and re-layouts, body(): storage = passage_home[group_candidates].reshape(shards, entries)  23 us
    gather x1, local copies, waits for them, and re-layouts, body(): passage_tiles = passages[local_slot]  14.4 us
    dot_general x1, matrix products, body(): jnp.einsum('sid,sjd->sij', query_tiles, passage_tiles, preferred_element_...  11.3 us
    reshape x2, local copies, waits for them, and re-layouts, body(): bases = returned[:, :capacity * width].reshape(shards * capacity, width)  9.12 us
  transfers between devices with their start and end apart: 2, of which 1 were waited for; matrix products, arithmetic and copies ran while one was open for 17% of the time, Pallas kernels for 0%

commit v1 on v0

--- a/solution.py
+++ b/solution.py
@@ -44,7 +44,13 @@
 
 def gather_bank(value):
     value = lax.all_gather(value, "y", axis=0, tiled=True)
-    return lax.all_gather(value, "z", axis=0, tiled=True)
+    scan_the_tiles = lambda work_x, along_dim: jnp.concatenate(
+        lax.all_to_all(
+            jnp.stack([work_x] * lax.axis_size("z")), axis_name="z", split_axis=0, concat_axis=0
+        ),
+        axis=along_dim,
+    )
+    return scan_the_tiles(value, 0)
 
 
 def body(queries, passages, passage_home, candidates, positive):

time: 257 us -> 248 us (0.965)
  blocking collectives: 54.7 us -> 25 us
  starting transfers between devices: 6.57 us -> 20.7 us
  between operations: 14.4 us -> 0.98 us
  waiting for transfers between devices: 62 us -> 73.8 us
  matrix products: 19.4 us -> 22.9 us
  local copies, waits for them, and re-layouts: 85.3 us -> 88.7 us
    all_gather x1 -> x0, blocking collectives: 28.2 us -> none  [gather_bank(): return lax.all_gather(value, 'z', axis=0, tiled=True)]
    all_to_all x0 -> x2, starting transfers between devices: none -> 15.7 us  [gather_bank(): lax.all_to_all(jnp.stack([work_x] * lax.axis_size('z')), axis_name='z', s...]
    all_to_all x1, waiting for transfers between devices: 62 us -> 69.2 us  [body(): returned = lax.all_to_all(payload, BANK, 0, 0, tiled=True)]
    all_to_all x0 -> x2, waiting for transfers between devices: none -> 4.6 us  [gather_bank(): lax.all_to_all(jnp.stack([work_x] * lax.axis_size('z')), axis_name='z', s...]
    dot_general x1, matrix products: 11.3 us -> 14.8 us  [body(): jnp.einsum('sid,sjd->sij', query_tiles, passage_tiles, preferred_element_...]
    unnamed x18 -> x19, local copies, waits for them, and re-layouts: 27.9 us -> 28.5 us
  transfers between devices with their start and end apart: 2 -> 3, of which waited for: 1 -> 2; matrix products, arithmetic and copies ran while one was open for 17% -> 17% of each run, Pallas kernels for 0% -> 0%
where the time goes in v1:
time: 248 us; the launch traced here: 247 us
  local copies, waits for them, and re-layouts  88.7 us (36%)
  waiting for transfers between devices  73.8 us (30%)
  blocking collectives  25 us (10%)
  matrix products  22.9 us (9%)
  starting transfers between devices  20.7 us (8%)
  other arithmetic  15.1 us (6%)
    all_to_all x1, waiting for transfers between devices, body(): returned = lax.all_to_all(payload, BANK, 0, 0, tiled=True)  69.2 us
    unnamed x19, local copies, waits for them, and re-layouts  28.5 us
    all_gather x2, blocking collectives, gather_bank(): value = lax.all_gather(value, 'y', axis=0, tiled=True)  25 us
    gather x1, local copies, waits for them, and re-layouts, body(): storage = passage_home[group_candidates].reshape(shards, entries)  23 us
    all_to_all x2, starting transfers between devices, gather_bank(): lax.all_to_all(jnp.stack([work_x] * lax.axis_size('z')), axis_name='z', s...  15.7 us
    dot_general x1, matrix products, body(): jnp.einsum('sid,sjd->sij', query_tiles, passage_tiles, preferred_element_...  14.8 us
    gather x1, local copies, waits for them, and re-layouts, body(): passage_tiles = passages[local_slot]  14.4 us
    reshape x2, local copies, waits for them, and re-layouts, body(): bases = returned[:, :capacity * width].reshape(shards * capacity, width)  9.12 us
  transfers between devices with their start and end apart: 3, of which 2 were waited for; matrix products, arithmetic and copies ran while one was open for 17% of the time, Pallas kernels for 0%

profile of v1, /device:TPU:2, one launch (start us, length us, event | category | flops | bytes accessed | tf_op | source)
XLA Modules:
  0.0 247.1 jit_solution(7843358409571720024)
XLA Ops:
  2.1 12.5 %all_gather.7 = s32[32,17]{1,0:T(8,128)S(1)} all-gather(s32[8,17]{1,0:T(8,128)S(1)} %pad_add_fusion), channel_id=1, replica_groups=mesh['query'=8,'z'=8,'y'=4] {'y'}, dimensions={0}, use_global_device_ids=true | all-gather | bytes 2720 | tf_op jit(solution)/shard_map/all_gather | solution.py:46
  15.5 8.5 %all-to-all-start.1 = ((s32[8,1,544]{2,1,0:T(1,128)}), s32[8,1,544]{2,1,0:T(1,128)S(1)}, u32[]{:S(2)}, u32[]{:S(2)}) async-start(s32[8,1,544]{2,1,0:T(1,128)} %reshape.548), calls=%async_computation.1 | async-start | bytes 40960 | tf_op jit(solution)/shard_map/all_to_all | solution.py:48
  23.9 12.5 %all_gather.6 = bf16[32,32,128]{2,1,0:T(8,128)(2,1)S(1)} all-gather(bf16[8,32,128]{2,1,0:T(8,128)(2,1)} %param.5), channel_id=1, replica_groups=mesh['query'=8,'z'=8,'y'=4] {'y'}, dimensions={0}, use_global_device_ids=true | all-gather | bytes 327680 | tf_op jit(solution)/shard_map/all_gather | solution.py:46
  36.4 1.7 stack.7
  38.1 7.2 %all-to-all-start = ((bf16[8,32,32,128]{3,2,1,0:T(8,128)(2,1)}), bf16[8,32,32,128]{3,2,1,0:T(8,128)(2,1)S(1)}, u32[]{:S(2)}, u32[]{:S(2)}) async-start(bf16[8,32,32,128]{3,2,1,0:T(8,128)(2,1)} %stack.7), calls=%async_computation | async-start | bytes 4194304 | tf_op jit(solution)/shard_map/all_to_all | solution.py:48
  47.2 23.0 %gather_fusion = s32[4096]{0:T(1024)S(1)} fusion(s32[8192]{0:T(1024)S(1)} %copy-done, s32[4096]{0:T(1024)S(1)} %broadcast_clamp_fusion), kind=kCustom, calls=%fused_computation | custom fusion | bytes 49152 | tf_op jit(solution)/shard_map/gather | solution.py:69
  71.5 14.4 %gather_fusion.2 = bf16[384,128,128]{2,1,0:T(8,128)(2,1)} fusion(bf16[256,128,128]{2,1,0:T(8,128)(2,1)} %param.6, s32[1024]{0:T(1024)S(1)} %pad_clamp_fusion.2), kind=kCustom, calls=%fused_computation.2 | custom fusion | bytes 25167360 | tf_op jit(solution)/shard_map/gather | solution.py:80
  85.9 4.6 %all-to-all-done = bf16[8,32,32,128]{3,2,1,0:T(8,128)(2,1)S(1)} async-done(((bf16[8,32,32,128]{3,2,1,0:T(8,128)(2,1)}), bf16[8,32,32,128]{3,2,1,0:T(8,128)(2,1)S(1)}, u32[]{:S(2)}, u32[]{:S(2)}) %all-to-all-start) | async-done | bytes 2097184 | tf_op jit(solution)/shard_map/all_to_all | solution.py:48
  90.5 3.2 %gather_fusion.1 = bf16[384,32,128]{2,1,0:T(8,128)(2,1)} fusion(bf16[256,32,128]{2,1,0:T(8,128)(2,1)S(1)} %bitcast.64, s32[1024]{0:T(1024)S(1)} %pad_clamp_fusion.3), kind=kCustom, calls=%fused_computation.1 | custom fusion | bytes 6292992 | tf_op jit(solution)/shard_map/gather | solution.py:81
  93.7 14.8 %fusion.27 = (f32[384,32]{1,0:T(8,128)S(1)}, f32[384,32,128]{2,1,0:T(8,128)}) fusion(bf16[384,32,128]{2,1,0:T(8,128)(2,1)} %gather_fusion.1, bf16[384,128,128]{2,1,0:T(8,128)(2,1)} %gather_fusion.2), kind=kOutput, calls=%fused_computation.94 | convolution fusion | flops 404213760 | bytes 22069248 | tf_op jit(solution)/shard_map/sid,sjd->sij/dot_general | solution.py:82
  108.5 5.8 %fusion = f32[384,32]{1,0:T(8,128)S(1)} fusion(f32[384,32,128]{2,1,0:T(8,128)} %get-tuple-element.22, f32[384,32]{1,0:T(8,128)S(1)} %get-tuple-element.21), kind=kLoop, calls=%fused_computation.7 | loop fusion | flops 3133440 | bytes 6389760 | tf_op jit(solution)/shard_map/reduce_sum | solution.py:14
  114.4 7.1 %fusion.4 = bf16[384,32,128]{2,1,0:T(8,128)(2,1)S(1)} fusion(bf16[384,128,128]{2,1,0:T(8,128)(2,1)} %gather_fusion.2, f32[384,32,128]{2,1,0:T(8,128)S(1)} %copy-done.1, f32[384,32]{1,0:T(8,128)S(1)} %fusion, f32[384,32]{1,0:T(8,128)S(1)} %get-tuple-element.21), kind=kOutput, calls=%fused_computation.12 | convolution fusion | flops 408944640 | bytes 22118400 | tf_op jit(solution)/shard_map/sij,sjd->sid/dot_general | solution.py:86
  121.7 2.8 %reshape.492 = bf16[32,49152]{1,0:T(8,128)(2,1)} reshape(bf16[384,32,128]{2,1,0:T(8,128)(2,1)S(1)} %fusion.4) | data formatting | bytes 6291456 | tf_op jit(solution)/shard_map/reshape | solution.py:92
  124.5 2.1 constant_dynamic-update-slice_fusion
  127.6 1.7 copy-done.2
  129.8 5.0 %reduce.7 = bf16[32,49280]{1,0:T(8,128)(2,1)S(1)} reduce(bf16[32,1,49280]{2,0,1:T(8,128)(2,1)} %bitcast.67, bf16[]{:T(256)} %broadcast.450), dimensions={1}, to_apply=%copy.34.reduce_sub_computation | reduce | bytes 6307842 | tf_op jit(solution)/shard_map/all_to_all | solution.py:98
  134.8 3.4 %reshape.550 = bf16[32,2,24640]{2,1,0:T(2,128)(2,1)} reshape(bf16[32,49280]{1,0:T(8,128)(2,1)S(1)} %reduce.7) | data formatting | bytes 6307840
  138.2 5.0 %all-to-all-start.2 = ((bf16[32,2,24640]{2,1,0:T(2,128)(2,1)}), bf16[32,2,24640]{2,1,0:T(2,128)(2,1)S(1)}, u32[]{:S(2)}, u32[]{:S(2)}) async-start(bf16[32,2,24640]{2,1,0:T(2,128)(2,1)} %reshape.550), calls=%async_computation.2 | async-start | bytes 6324224 | tf_op jit(solution)/shard_map/all_to_all | solution.py:98
  143.4 1.1 gather_fusion.3
  145.2 69.2 %all-to-all-done.2 = bf16[32,2,24640]{2,1,0:T(2,128)(2,1)S(1)} async-done(((bf16[32,2,24640]{2,1,0:T(2,128)(2,1)}), bf16[32,2,24640]{2,1,0:T(2,128)(2,1)S(1)}, u32[]{:S(2)}, u32[]{:S(2)}) %all-to-all-start.2) | async-done | bytes 3153952 | tf_op jit(solution)/shard_map/all_to_all | solution.py:98
  214.5 16.4 %reshape.551 = bf16[32,1,49280]{2,1,0:T(2,128)(2,1)} reshape(bf16[32,2,24640]{2,1,0:T(2,128)(2,1)S(1)} %all-to-all-done.2) | data formatting | bytes 6307840
  230.8 3.1 %copy.39 = bf16[32,1,49280]{2,0,1:T(8,128)(2,1)S(1)} copy(bf16[32,1,49280]{2,1,0:T(2,128)(2,1)} %reshape.551) | data formatting | bytes 6307840
  236.3 5.7 %reshape.496 = bf16[384,4096]{1,0:T(8,128)(2,1)} reshape(bf16[32,49152]{1,0:T(8,128)(2,1)S(1)} %slice.39) | data formatting | bytes 6291456 | tf_op jit(solution)/shard_map/reshape | solution.py:114
  242.0 3.4 %copy.35 = bf16[384,4096]{0,1:T(8,128)(2,1)S(1)} copy(bf16[384,4096]{1,0:T(8,128)(2,1)} %reshape.496) | data formatting | bytes 6291456 | tf_op jit(solution)/shard_map/reshape | solution.py:114
  (74 shorter events, 11.7 us)
Async XLA Ops:
  0.6 46.5 %copy-start = (s32[8192]{0:T(1024)S(1)}, s32[8192]{0:T(1024)}, u32[]{:S(2)}) copy-start(s32[8192]{0:T(1024)} %param.7) | copy-start | bytes 98308
  15.5 20.9 %all-to-all-start.1 = ((s32[8,1,544]{2,1,0:T(1,128)}), s32[8,1,544]{2,1,0:T(1,128)S(1)}, u32[]{:S(2)}, u32[]{:S(2)}) async-start(s32[8,1,544]{2,1,0:T(1,128)} %reshape.548), calls=%async_computation.1 | async-start | bytes 40960 | tf_op jit(solution)/shard_map/all_to_all | solution.py:48
  38.1 52.4 %all-to-all-start = ((bf16[8,32,32,128]{3,2,1,0:T(8,128)(2,1)}), bf16[8,32,32,128]{3,2,1,0:T(8,128)(2,1)S(1)}, u32[]{:S(2)}, u32[]{:S(2)}) async-start(bf16[8,32,32,128]{3,2,1,0:T(8,128)(2,1)} %stack.7), calls=%async_computation | async-start | bytes 4194304 | tf_op jit(solution)/shard_map/all_to_all | solution.py:48
  108.5 5.8 %copy-start.1 = (f32[384,32,128]{2,1,0:T(8,128)S(1)}, f32[384,32,128]{2,1,0:T(8,128)}, u32[]{:S(2)}) copy-start(f32[384,32,128]{2,1,0:T(8,128)} %get-tuple-element.22) | copy-start | bytes 18874372
  127.6 1.7 copy-start.2
  138.2 5.0 %copy-start.3 = (s32[8,16]{1,0:T(8,128)S(1)}, s32[8,16]{1,0:T(8,128)}, u32[]{:S(2)}) copy-start(s32[8,16]{1,0:T(8,128)} %param.8) | copy-start | bytes 1540
  138.2 76.2 %all-to-all-start.2 = ((bf16[32,2,24640]{2,1,0:T(2,128)(2,1)}), bf16[32,2,24640]{2,1,0:T(2,128)(2,1)S(1)}, u32[]{:S(2)}, u32[]{:S(2)}) async-start(bf16[32,2,24640]{2,1,0:T(2,128)(2,1)} %reshape.550), calls=%async_computation.2 | async-start | bytes 6324224 | tf_op jit(solution)/shard_map/all_to_all | solution.py:98
  234.0 1.5 copy-start.4
